TPU v7x, 32 devices: a whole 2x2x4 slice. The times are simulated.
32 devices in a mesh: dom: 8 (over z, core), loop: 4 (over y, x).
Axes of the slice: x: 2, y: 2, z: 4, core: 2. Of those that a mesh axis runs over, the one named last changes fastest.
Arguments:
- cotangent: bfloat16 [32768, 256], P(('dom', 'loop')), may hold values from -6 to 6
- preact: bfloat16 [32768, 256], P(('dom', 'loop')), may hold values from -6 to 6
- aggregated: bfloat16 [32768, 256], P(('dom', 'loop')), may hold values from -6 to 6
- weight: bfloat16 [256, 256], replicated, may hold values from -0.375 to 0.375
- tile_values: bfloat16 [20480, 128, 128], P(('dom', 'loop')), as said below
- tile_rows: int32 [32, 640], P(('dom', 'loop')), may hold values from 0 to 31
- tile_cols: int32 [32, 640], P(('dom', 'loop')), may hold values from 0 to 63, as said below
- tile_counts: int32 [32], P(('dom', 'loop')), may hold values from 32 to 640
Outputs:
- node_grad: float32 [32768, 256], P(('dom', 'loop'))
- weight_grad: float32 [256, 256], replicated
Inputs may be any that keep to these rules, and one draw needn't show every extreme that they name: `tile_cols`: the live tiles of one device touch, for every dom index, exactly 4 distinct column blocks, and every tile's column lies among them. `tile_values`: entries are nonnegative.
All inputs are finite; a program needn't handle non-finite values.
Results may differ from a plain program's by a relative error of at most 0.0029.
Values may be sent and summed in bfloat16 or wider, within the bound.
No kernel may reach another device: no remote copies, remote signals or barrier semaphores. Data moves between devices by JAX's collectives and lax.ppermute only.
A program may use at most 192 MiB of HBM per device.

v0:
```python
import math

import jax
import jax.numpy as jnp
from jax import lax
from jax.experimental import pallas as pl
from jax.experimental.pallas import tpu as pltpu
from jax.sharding import PartitionSpec as P

GROUP = 32
CAP = 4


def _spmm_kernel(rows_ref, slots_ref, cnt_ref, tv_ref, part_ref, extra_ref, out_ref):
    g = pl.program_id(0)
    count = cnt_ref[0]
    group, tile_size, _ = tv_ref.shape
    base = g * group
    body_rows = CAP * tile_size

    @pl.when(g == 0)
    def _():
        out_ref[:, :body_rows, :] = jnp.zeros(
            (out_ref.shape[0], body_rows, out_ref.shape[2]), out_ref.dtype
        )
        out_ref[:, body_rows:, :] = extra_ref[...]

    @pl.when(base < count)
    def _():
        for t in range(group):
            j = base + t
            r = rows_ref[j]
            c = slots_ref[j]
            term = lax.dot_general(
                tv_ref[t],
                part_ref[r],
                (((0,), (0,)), ((), ())),
                preferred_element_type=jnp.float32,
            )
            dest = c // CAP
            start = pl.multiple_of((c % CAP) * tile_size, tile_size)
            window = out_ref.at[dest, pl.ds(start, tile_size), :]
            window[...] += jnp.where(j < count, term, 0.0)


def _spmm(rows, slots, count, tile_values, partition, extra):
    tiles, tile_size, _ = tile_values.shape
    part_blocks, _, width = partition.shape
    dests, extra_rows, _ = extra.shape
    out_rows = CAP * tile_size + extra_rows
    group = math.gcd(tiles, GROUP)

    def tv_map(g, rows_ref, slots_ref, cnt_ref):
        last = jnp.maximum((cnt_ref[0] + group - 1) // group - 1, 0)
        return (jnp.minimum(g, last), 0, 0)

    def whole(g, rows_ref, slots_ref, cnt_ref):
        return (0, 0, 0)

    return pl.pallas_call(
        _spmm_kernel,
        out_shape=jax.ShapeDtypeStruct((dests, out_rows, width), jnp.float32),
        grid_spec=pltpu.PrefetchScalarGridSpec(
            num_scalar_prefetch=3,
            grid=(tiles // group,),
            in_specs=[
                pl.BlockSpec((group, tile_size, tile_size), tv_map),
                pl.BlockSpec((part_blocks, tile_size, width), whole),
                pl.BlockSpec((dests, extra_rows, width), whole),
            ],
            out_specs=pl.BlockSpec((dests, out_rows, width), whole),
        ),
        compiler_params=pltpu.CompilerParams(
            dimension_semantics=("arbitrary",),
            vmem_limit_bytes=50 * 1024 * 1024,
        ),
        cost_estimate=pl.CostEstimate(
            flops=2 * tiles * tile_size * tile_size * width,
            transcendentals=0,
            bytes_accessed=tiles * tile_size * tile_size * 2 + dests * out_rows * width * 4,
        ),
    )(rows, slots, count, tile_values, partition, extra)


def _combine_kernel(map_ref, *refs):
    slab_refs = refs[:-2]
    init_ref, out_ref = refs[-2:]
    out_blocks, tile_size, width = out_ref.shape
    out_ref[...] = init_ref[...].reshape(out_blocks, tile_size, width)
    for n, slab_ref in enumerate(slab_refs):
        for k in range(CAP):
            b = map_ref[n * CAP + k]
            out_ref[b] += slab_ref[k * tile_size:(k + 1) * tile_size, :]


def _combine(block_map, slabs, init, out_blocks, tile_size):
    rows, width = slabs[0].shape

    def whole(g, map_ref):
        return (0, 0)

    def out_map(g, map_ref):
        return (0, 0, 0)

    return pl.pallas_call(
        _combine_kernel,
        out_shape=jax.ShapeDtypeStruct((out_blocks, tile_size, width), jnp.float32),
        grid_spec=pltpu.PrefetchScalarGridSpec(
            num_scalar_prefetch=1,
            grid=(1,),
            in_specs=[pl.BlockSpec((rows, width), whole) for _ in slabs]
            + [pl.BlockSpec((out_blocks * tile_size, width), whole)],
            out_specs=pl.BlockSpec((out_blocks, tile_size, width), out_map),
        ),
        compiler_params=pltpu.CompilerParams(dimension_semantics=("arbitrary",)),
        cost_estimate=pl.CostEstimate(
            flops=len(slabs) * CAP * tile_size * width,
            transcendentals=0,
            bytes_accessed=(len(slabs) * CAP + 2 * out_blocks) * tile_size * width * 4,
        ),
    )(block_map, *slabs, init)


def _pick(stacked, index):
    return lax.dynamic_index_in_dim(stacked, index, axis=0, keepdims=False)


def shards(cotangent, preact, aggregated, weight, tile_values, tile_rows, tile_cols, tile_counts):
    node_rows, width = cotangent.shape
    tile_size = tile_values.shape[1]
    dom_count = lax.axis_size("dom")
    loop_count = lax.axis_size("loop")
    dom_index = lax.axis_index("dom")
    loop_index = lax.axis_index("loop")
    total_nodes = node_rows * dom_count * loop_count
    local_blocks = node_rows // tile_size
    tile_total = tile_rows.shape[1]

    masked = jnp.where(preact > 0, cotangent, jnp.zeros_like(cotangent))
    weight_term = jnp.dot(aggregated.T, masked, preferred_element_type=jnp.float32) * (
        1.0 / math.sqrt(total_nodes)
    )
    projected = jnp.dot(masked, weight.T, preferred_element_type=jnp.float32).astype(jnp.bfloat16)

    pieces = [projected]
    for shift in range(1, loop_count):
        pairs = [(i, (i + shift) % loop_count) for i in range(loop_count)]
        pieces.append(lax.ppermute(projected, "loop", pairs))
    partition = jnp.concatenate(pieces, axis=0).reshape(
        loop_count * local_blocks, tile_size, width
    )
    partition, weight_term = lax.optimization_barrier((partition, weight_term))
    terms = [weight_term]
    for shift in range(1, loop_count):
        pairs = [(i, (i + shift) % loop_count) for i in range(loop_count)]
        terms.append(lax.ppermute(weight_term, "loop", pairs))
    terms = jnp.stack(terms)
    loop_sum = _pick(terms, loop_index % loop_count)
    for source in range(1, loop_count):
        loop_sum = loop_sum + _pick(terms, (loop_index - source) % loop_count)

    rows = tile_rows[0]
    source_loop = rows // local_blocks
    rows = ((loop_index - source_loop) % loop_count) * local_blocks + rows % local_blocks

    cols = tile_cols[0]
    live = jnp.arange(tile_total, dtype=jnp.int32) < tile_counts[0]
    all_blocks = dom_count * local_blocks
    onehot = cols[:, None] == jnp.arange(all_blocks, dtype=jnp.int32)[None, :]
    present = jnp.any(onehot & live[:, None], axis=0).reshape(dom_count, local_blocks)
    present = present.astype(jnp.int32)
    rank = jnp.cumsum(present, axis=1) - 1
    tile_rank = jnp.sum(jnp.where(onehot, rank.reshape(1, -1), 0), axis=1)
    tile_rank = jnp.clip(tile_rank, 0, CAP - 1)
    block_ids = jnp.arange(local_blocks, dtype=jnp.int32)
    table = jnp.stack(
        [jnp.sum(jnp.where((rank == k) & (present > 0), block_ids[None, :], 0), axis=1) for k in range(CAP)],
        axis=1,
    )
    half = dom_count // 2
    side = dom_index // half
    pos = dom_index % half
    dest_dom = cols // local_blocks
    cross = (dest_dom // half != side).astype(jnp.int32)
    slots = (cross * half + (dest_dom % half - pos) % half) * CAP + tile_rank
    order = jnp.arange(dom_count, dtype=jnp.int32)
    order_side = jnp.where(order // half == 0, side, 1 - side)
    order = order_side * half + (pos + order % half) % half
    dom_ids = jnp.arange(dom_count, dtype=jnp.int32)
    rotate = order[:, None] == dom_ids[None, :]
    table = jnp.sum(jnp.where(rotate[:, :, None], table[None, :, :], 0), axis=1)

    id_rows = jnp.zeros((dom_count, 8, width), jnp.float32)
    extra = id_rows.at[:, 0, :CAP].set(table.astype(jnp.float32))

    compact = _spmm(rows, slots, tile_counts, tile_values, partition, extra)
    body_rows = CAP * tile_size
    chunk = width // dom_count
    chunks = loop_sum.reshape(dom_count, chunk, width)
    first = [_pick(chunks, order[half + i]) for i in range(half)]
    second = [_pick(chunks, order[i]) for i in range(half)]

    def within(shift):
        return [(i, (i // half) * half + (i % half + shift) % half) for i in range(dom_count)]

    swap = [(i, (1 - i // half) * half + i % half) for i in range(dom_count)]

    def ids_of(slabs):
        return jnp.concatenate([slab[body_rows, :CAP] for slab in slabs]).astype(jnp.int32)

    relay = [compact[half]]
    relay_chunk = first[0]
    own = second[0]
    for shift in range(1, half):
        slab, pair = lax.ppermute(
            (compact[half + shift], jnp.stack([first[shift], second[shift]])), "dom", within(shift)
        )
        relay.append(slab)
        relay_chunk = relay_chunk + pair[0]
        own = own + pair[1]
    own = own + lax.ppermute(relay_chunk, "dom", swap)
    zeros = jnp.zeros((local_blocks * tile_size, width), jnp.float32)
    payload = _combine(ids_of(relay), relay, zeros, local_blocks, tile_size)

    held = [own]
    for shift in range(1, half):
        held.append(lax.ppermute(own, "dom", within(shift)))
    held = jnp.stack(held)
    half_chunks = jnp.concatenate(
        [_pick(held, (pos - q) % half) for q in range(half)], axis=0
    )
    payload = jnp.concatenate([payload.reshape(node_rows, width), half_chunks], axis=0)

    direct = [compact[shift] for shift in range(1, half)]
    direct, payload = lax.optimization_barrier((direct, payload))
    partner = lax.ppermute(payload, "dom", swap)
    received = [compact[0]]
    for shift in range(1, half):
        received.append(lax.ppermute(direct[shift - 1], "dom", within(shift)))
    node_grad = _combine(ids_of(received), received, partner, local_blocks, tile_size)
    node_grad = node_grad.reshape(node_rows, width)
    other_chunks = partner[node_rows:]
    weight_grad = jnp.where(
        side == 0,
        jnp.concatenate([half_chunks, other_chunks], axis=0),
        jnp.concatenate([other_chunks, half_chunks], axis=0),
    )
    return (node_grad, weight_grad)


def solution(mesh):
    return jax.shard_map(
        shards,
        mesh=mesh,
        in_specs=(
            P(("dom", "loop"), None),
            P(("dom", "loop"), None),
            P(("dom", "loop"), None),
            P(),
            P(("dom", "loop"), None, None),
            P(("dom", "loop"), None),
            P(("dom", "loop"), None),
            P(("dom", "loop")),
        ),
        out_specs=(P(("dom", "loop"), None), P()),
        check_vma=False,
    )
```

profile of v0, /device:TPU:0, one launch (start us, length us, event | category | flops | bytes accessed | tf_op | source)
XLA Modules:
  0.0 180.6 jit_solution(12805122574335049592)
XLA Ops:
  0.7 1.7 convolution_convert_fusion
  2.4 3.0 %collective-permute-start = (bf16[1024,256]{1,0:T(8,128)(2,1)S(1)}, bf16[1024,256]{1,0:T(8,128)(2,1)}, u32[]{:S(2)}, u32[]{:S(2)}) collective-permute-start(bf16[1024,256]{1,0:T(8,128)(2,1)S(1)} %convolution_convert_fusion), channel_id=1, source_target_pairs={{0,1},{1,2},{2,3},{3,0},{4,5},{5,6},{6,7},{7,4},{8,9},{9,10},{10,1... | collective-permute-start | bytes 1572872 | tf_op jit(solution)/shard_map/ppermute | solution.py:148
  5.3 1.5 collective-permute-start.1
  6.9 1.4 collective-permute-start.2
  10.4 8.8 %collective-permute-done = bf16[1024,256]{1,0:T(8,128)(2,1)} collective-permute-done((bf16[1024,256]{1,0:T(8,128)(2,1)S(1)}, bf16[1024,256]{1,0:T(8,128)(2,1)}, u32[]{:S(2)}, u32[]{:S(2)}) %collective-permute-start) | collective-permute-done | bytes 524320 | tf_op jit(solution)/shard_map/ppermute | solution.py:148
  19.2 10.4 %collective-permute-done.1 = bf16[1024,256]{1,0:T(8,128)(2,1)} collective-permute-done((bf16[1024,256]{1,0:T(8,128)(2,1)S(1)}, bf16[1024,256]{1,0:T(8,128)(2,1)}, u32[]{:S(2)}, u32[]{:S(2)}) %collective-permute-start.1) | collective-permute-done | bytes 524320 | tf_op jit(solution)/shard_map/ppermute | solution.py:148
  29.8 1.5 pad_maximum_fusion
  31.3 1.8 collective-permute-start.6
  33.5 2.2 %collective-permute-start.8 = (f32[256,256]{0,1:T(8,128)S(1)}, f32[256,256]{0,1:T(8,128)}, u32[]{:S(2)}, u32[]{:S(2)}) collective-permute-start(f32[256,256]{0,1:T(8,128)S(1)} %fusion), channel_id=1, source_target_pairs={{0,3},{1,0},{2,1},{3,2},{4,7},{5,4},{6,5},{7,6},{8,11},{9,8},{10,9... | collective-permute-start | bytes 786440 | tf_op jit(solution)/shard_map/ppermute | solution.py:156
  53.0 1.6 collective-permute-start.10
  56.0 19.5 %shard_map.95 = f32[8,520,256]{2,1,0:T(8,128)} custom-call(s32[640]{0:T(1024)S(1)} %get-tuple-element.63.rows_ref, s32[640]{0:T(1024)S(1)} %get-tuple-element.64.slots_ref, s32[1]{0:T(128)} %copy.37.cnt_ref, bf16[640,128,128]{2,1,0:T(8,128)(2,1)} %tv_ref.1, bf16[32,128,256]{2,1,0:T(8,128)(2,1)S(1)} %bitcast.86, f32[8,8,256]{2,1,0:T(8,128)S(1)} %scatter.4.extra_ref), custom_call_target="tpu_custom_call" | custom-call | flops 5368709120 | bytes 25231360 | tf_op jit(solution)/shard_map/pallas_call | solution.py:60
  75.6 3.6 %slice_bitcast_fusion.7 = (f32[520,256]{1,0:T(8,128)S(1)}, f32[520,256]{1,0:T(8,128)S(1)}, f32[520,256]{1,0:T(8,128)S(1)}, f32[520,256]{1,0:T(8,128)S(1)}, f32[5...) fusion(f32[8,520,256]{2,1,0:T(8,128)} %shard_map.95), kind=kLoop, calls=%fused_computation.13 | loop fusion | bytes 8519680 | tf_op jit(solution)/shard_map/squeeze | solution.py:237
  79.2 7.3 %collective-permute-start.5 = (f32[520,256]{1,0:T(8,128)S(1)}, f32[520,256]{1,0:T(8,128)S(1)}, u32[]{:S(2)}, u32[]{:S(2)}) collective-permute-start(f32[520,256]{1,0:T(8,128)S(1)} %get-tuple-element.31), channel_id=1, source_target_pairs={{0,12},{4,0},{8,4},{12,8},{16,28},{20,16},{24,20},{28,24},{1,13},{... | collective-permute-start | bytes 1597448 | tf_op jit(solution)/shard_map/ppermute | solution.py:215
  86.8 1.9 %collective-permute-start.14 = (f32[32,256]{1,0:T(8,128)S(1)}, f32[32,256]{1,0:T(8,128)S(1)}, u32[]{:S(2)}, u32[]{:S(2)}) collective-permute-start(f32[32,256]{1,0:T(8,128)S(1)} %fusion.5), channel_id=1, source_target_pairs={{0,8},{4,12},{8,0},{12,4},{16,24},{20,28},{24,16},{28,20},{1,9},{5... | collective-permute-start | bytes 98312 | tf_op jit(solution)/shard_map/ppermute | solution.py:227
  90.1 9.9 %collective-permute-done.13 = f32[32,256]{1,0:T(8,128)S(1)} collective-permute-done((f32[32,256]{1,0:T(8,128)S(1)}, f32[32,256]{1,0:T(8,128)S(1)}, u32[]{:S(2)}, u32[]{:S(2)}) %collective-permute-start.13) | collective-permute-done | bytes 32800 | tf_op jit(solution)/shard_map/ppermute | solution.py:227
  100.0 8.7 %collective-permute-done.14 = f32[32,256]{1,0:T(8,128)S(1)} collective-permute-done((f32[32,256]{1,0:T(8,128)S(1)}, f32[32,256]{1,0:T(8,128)S(1)}, u32[]{:S(2)}, u32[]{:S(2)}) %collective-permute-start.14) | collective-permute-done | bytes 32800 | tf_op jit(solution)/shard_map/ppermute | solution.py:227
  112.1 3.8 %shard_map.96 = f32[8,128,256]{2,1,0:T(8,128)} custom-call(s32[16]{0:T(128)} %maximum_convert_fusion.map_ref, f32[520,256]{1,0:T(8,128)} %copy-done.2, f32[520,256]{1,0:T(8,128)} %copy-done.7, f32[520,256]{1,0:T(8,128)} %copy-done.5, f32[520,256]{1,0:T(8,128)} %copy-done.4, f32[1024,256]{1,0:T(8,128)} %broadcast_in_dim.81.refs_4_), custom_call_target="tpu_custom_call" | custom-call | flops 524288 | bytes 4194304 | tf_op jit(solution)/shard_map/pallas_call | solution.py:105
  122.1 2.8 %collective-permute-start.17 = (f32[520,256]{1,0:T(8,128)}, f32[520,256]{1,0:T(8,128)S(1)}, u32[]{:S(2)}, u32[]{:S(2)}) collective-permute-start(f32[520,256]{1,0:T(8,128)} %get-tuple-element.23), channel_id=1, source_target_pairs={{0,8},{4,12},{8,0},{12,4},{16,24},{20,28},{24,16},{28,20},{1,9},{5... | collective-permute-start | bytes 1597448 | tf_op jit(solution)/shard_map/ppermute | solution.py:239
  124.9 11.6 %collective-permute-done.16.refs_1_ = f32[520,256]{1,0:T(8,128)} collective-permute-done((f32[520,256]{1,0:T(8,128)}, f32[520,256]{1,0:T(8,128)}, u32[]{:S(2)}, u32[]{:S(2)}) %collective-permute-start.16) | collective-permute-done | bytes 532512 | tf_op jit(solution)/shard_map/ppermute | solution.py:239
  137.2 20.1 %collective-permute-done.18.refs_3_ = f32[520,256]{1,0:T(8,128)} collective-permute-done((f32[520,256]{1,0:T(8,128)}, f32[520,256]{1,0:T(8,128)}, u32[]{:S(2)}, u32[]{:S(2)}) %collective-permute-start.18) | collective-permute-done | bytes 532512 | tf_op jit(solution)/shard_map/ppermute | solution.py:239
  157.9 10.7 %collective-permute-done.17.refs_2_ = f32[520,256]{1,0:T(8,128)S(1)} collective-permute-done((f32[520,256]{1,0:T(8,128)}, f32[520,256]{1,0:T(8,128)S(1)}, u32[]{:S(2)}, u32[]{:S(2)}) %collective-permute-start.17) | collective-permute-done | bytes 532512 | tf_op jit(solution)/shard_map/ppermute | solution.py:239
  169.4 5.0 %collective-permute-done.19.refs_4_ = f32[1152,256]{1,0:T(8,128)S(1)} collective-permute-done((f32[1152,256]{1,0:T(8,128)S(1)}, f32[1152,256]{1,0:T(8,128)S(1)}, u32[]{:S(2)}, u32[]{:S(2)}) %collective-permute-start.19) | collective-permute-done | bytes 1179680 | tf_op jit(solution)/shard_map/ppermute | solution.py:236
  175.1 1.7 broadcast_select_fusion
  176.8 3.8 %shard_map.97 = f32[8,128,256]{2,1,0:T(8,128)} custom-call(s32[16]{0:T(128)} %maximum_convert_fusion.1.map_ref, f32[520,256]{1,0:T(8,128)} %copy-done.1, f32[520,256]{1,0:T(8,128)} %collective-permute-done.16.refs_1_, f32[520,256]{1,0:T(8,128)} %copy-done.6, f32[520,256]{1,0:T(8,128)} %collective-permute-done.18.refs_3_, f32[1152,256]{1,0:T(8,128)} %copy-done.3), custom_call_target="tpu_custom_call" | custom-call | flops 524288 | bytes 4194304 | tf_op jit(solution)/shard_map/pallas_call | solution.py:105
  (98 shorter events, 19.7 us)
Async XLA Ops:
  0.6 9.3 %copy-start = (bf16[1024,256]{1,0:T(8,128)(2,1)S(1)}, bf16[1024,256]{1,0:T(8,128)(2,1)}, u32[]{:S(2)}) copy-start(bf16[1024,256]{1,0:T(8,128)(2,1)} %param.12) | copy-start | bytes 1572868
  2.4 16.9 %collective-permute-start = (bf16[1024,256]{1,0:T(8,128)(2,1)S(1)}, bf16[1024,256]{1,0:T(8,128)(2,1)}, u32[]{:S(2)}, u32[]{:S(2)}) collective-permute-start(bf16[1024,256]{1,0:T(8,128)(2,1)S(1)} %convolution_convert_fusion), channel_id=1, source_target_pairs={{0,1},{1,2},{2,3},{3,0},{4,5},{5,6},{6,7},{7,4},{8,9},{9,10},{10,1... | collective-permute-start | bytes 1572872 | tf_op jit(solution)/shard_map/ppermute | solution.py:148
  5.3 24.2 %collective-permute-start.1 = (bf16[1024,256]{1,0:T(8,128)(2,1)S(1)}, bf16[1024,256]{1,0:T(8,128)(2,1)}, u32[]{:S(2)}, u32[]{:S(2)}) collective-permute-start(bf16[1024,256]{1,0:T(8,128)(2,1)S(1)} %convolution_convert_fusion), channel_id=1, source_target_pairs={{0,2},{1,3},{2,0},{3,1},{4,6},{5,7},{6,4},{7,5},{8,10},{9,11},{10,... | collective-permute-start | bytes 1572872 | tf_op jit(solution)/shard_map/ppermute | solution.py:148
  6.9 23.0 %collective-permute-start.2 = (bf16[1024,256]{1,0:T(8,128)(2,1)S(1)}, bf16[1024,256]{1,0:T(8,128)(2,1)}, u32[]{:S(2)}, u32[]{:S(2)}) collective-permute-start(bf16[1024,256]{1,0:T(8,128)(2,1)S(1)} %convolution_convert_fusion), channel_id=1, source_target_pairs={{0,3},{1,0},{2,1},{3,2},{4,7},{5,4},{6,5},{7,6},{8,11},{9,8},{10,9... | collective-permute-start | bytes 1572872 | tf_op jit(solution)/shard_map/ppermute | solution.py:148
  10.4 36.0 %copy-start.9 = (s32[1,640]{1,0:T(1,128)S(1)}, s32[1,640]{1,0:T(1,128)}, u32[]{:S(2)}) copy-start(s32[1,640]{1,0:T(1,128)} %param.15) | copy-start | bytes 7684
  31.3 20.1 %collective-permute-start.6 = (f32[256,256]{0,1:T(8,128)S(1)}, f32[256,256]{0,1:T(8,128)S(1)}, u32[]{:S(2)}, u32[]{:S(2)}) collective-permute-start(f32[256,256]{0,1:T(8,128)S(1)} %fusion), channel_id=1, source_target_pairs={{0,1},{1,2},{2,3},{3,0},{4,5},{5,6},{6,7},{7,4},{8,9},{9,10},{10,1... | collective-permute-start | bytes 786440 | tf_op jit(solution)/shard_map/ppermute | solution.py:156
  33.1 18.4 %collective-permute-start.7 = (f32[256,256]{0,1:T(8,128)S(1)}, f32[256,256]{0,1:T(8,128)}, u32[]{:S(2)}, u32[]{:S(2)}) collective-permute-start(f32[256,256]{0,1:T(8,128)S(1)} %fusion), channel_id=1, source_target_pairs={{0,2},{1,3},{2,0},{3,1},{4,6},{5,7},{6,4},{7,5},{8,10},{9,11},{10,... | collective-permute-start | bytes 786440 | tf_op jit(solution)/shard_map/ppermute | solution.py:156
  33.5 18.0 %collective-permute-start.8 = (f32[256,256]{0,1:T(8,128)S(1)}, f32[256,256]{0,1:T(8,128)}, u32[]{:S(2)}, u32[]{:S(2)}) collective-permute-start(f32[256,256]{0,1:T(8,128)S(1)} %fusion), channel_id=1, source_target_pairs={{0,3},{1,0},{2,1},{3,2},{4,7},{5,4},{6,5},{7,6},{8,11},{9,8},{10,9... | collective-permute-start | bytes 786440 | tf_op jit(solution)/shard_map/ppermute | solution.py:156
  52.9 22.6 %collective-permute-start.9 = (f32[2,32,256]{2,1,0:T(8,128)S(1)}, f32[2,32,256]{2,1,0:T(8,128)S(1)}, u32[]{:S(2)}, u32[]{:S(2)}) collective-permute-start(f32[2,32,256]{2,1,0:T(8,128)S(1)} %pad_maximum_fusion.3), channel_id=1, source_target_pairs={{0,4},{4,8},{8,12},{12,0},{16,20},{20,24},{24,28},{28,16},{1,5},{5... | collective-permute-start | bytes 196616 | tf_op jit(solution)/shard_map/ppermute | solution.py:215
  53.0 22.6 %collective-permute-start.10 = (f32[2,32,256]{2,1,0:T(8,128)S(1)}, f32[2,32,256]{2,1,0:T(8,128)S(1)}, u32[]{:S(2)}, u32[]{:S(2)}) collective-permute-start(f32[2,32,256]{2,1,0:T(8,128)S(1)} %pad_maximum_fusion.4), channel_id=1, source_target_pairs={{0,8},{4,12},{8,0},{12,4},{16,24},{20,28},{24,16},{28,20},{1,9},{5... | collective-permute-start | bytes 196616 | tf_op jit(solution)/shard_map/ppermute | solution.py:215
  54.6 20.9 %collective-permute-start.11 = (f32[2,32,256]{2,1,0:T(8,128)S(1)}, f32[2,32,256]{2,1,0:T(8,128)S(1)}, u32[]{:S(2)}, u32[]{:S(2)}) collective-permute-start(f32[2,32,256]{2,1,0:T(8,128)S(1)} %pad_maximum_fusion.5), channel_id=1, source_target_pairs={{0,12},{4,0},{8,4},{12,8},{16,28},{20,16},{24,20},{28,24},{1,13},{... | collective-permute-start | bytes 196616 | tf_op jit(solution)/shard_map/ppermute | solution.py:215
  75.6 11.0 %collective-permute-start.12 = (f32[32,256]{1,0:T(8,128)S(1)}, f32[32,256]{1,0:T(8,128)S(1)}, u32[]{:S(2)}, u32[]{:S(2)}) collective-permute-start(f32[32,256]{1,0:T(8,128)S(1)} %fusion.3), channel_id=1, source_target_pairs={{0,16},{4,20},{8,24},{12,28},{16,0},{20,4},{24,8},{28,12},{1,17},{... | collective-permute-start | bytes 98312 | tf_op jit(solution)/shard_map/ppermute | solution.py:221
  79.2 32.8 %copy-start.2 = (f32[520,256]{1,0:T(8,128)}, f32[520,256]{1,0:T(8,128)S(1)}, u32[]{:S(2)}) copy-start(f32[520,256]{1,0:T(8,128)S(1)} %get-tuple-element.34.refs_0_) | copy-start | bytes 1597444
  79.2 45.7 %copy-start.1 = (f32[520,256]{1,0:T(8,128)}, f32[520,256]{1,0:T(8,128)S(1)}, u32[]{:S(2)}) copy-start(f32[520,256]{1,0:T(8,128)S(1)} %get-tuple-element.30.refs_0_) | copy-start | bytes 1597444
  79.2 30.2 %collective-permute-start.5 = (f32[520,256]{1,0:T(8,128)S(1)}, f32[520,256]{1,0:T(8,128)S(1)}, u32[]{:S(2)}, u32[]{:S(2)}) collective-permute-start(f32[520,256]{1,0:T(8,128)S(1)} %get-tuple-element.31), channel_id=1, source_target_pairs={{0,12},{4,0},{8,4},{12,8},{16,28},{20,16},{24,20},{28,24},{1,13},{... | collective-permute-start | bytes 1597448 | tf_op jit(solution)/shard_map/ppermute | solution.py:215
  86.5 22.9 %collective-permute-start.4 = (f32[520,256]{1,0:T(8,128)S(1)}, f32[520,256]{1,0:T(8,128)S(1)}, u32[]{:S(2)}, u32[]{:S(2)}) collective-permute-start(f32[520,256]{1,0:T(8,128)S(1)} %get-tuple-element.32), channel_id=1, source_target_pairs={{0,8},{4,12},{8,0},{12,4},{16,24},{20,28},{24,16},{28,20},{1,9},{5... | collective-permute-start | bytes 1597448 | tf_op jit(solution)/shard_map/ppermute | solution.py:215
  86.6 13.5 %collective-permute-start.13 = (f32[32,256]{1,0:T(8,128)S(1)}, f32[32,256]{1,0:T(8,128)S(1)}, u32[]{:S(2)}, u32[]{:S(2)}) collective-permute-start(f32[32,256]{1,0:T(8,128)S(1)} %fusion.5), channel_id=1, source_target_pairs={{0,4},{4,8},{8,12},{12,0},{16,20},{20,24},{24,28},{28,16},{1,5},{5... | collective-permute-start | bytes 98312 | tf_op jit(solution)/shard_map/ppermute | solution.py:227
  86.8 21.9 %collective-permute-start.14 = (f32[32,256]{1,0:T(8,128)S(1)}, f32[32,256]{1,0:T(8,128)S(1)}, u32[]{:S(2)}, u32[]{:S(2)}) collective-permute-start(f32[32,256]{1,0:T(8,128)S(1)} %fusion.5), channel_id=1, source_target_pairs={{0,8},{4,12},{8,0},{12,4},{16,24},{20,28},{24,16},{28,20},{1,9},{5... | collective-permute-start | bytes 98312 | tf_op jit(solution)/shard_map/ppermute | solution.py:227
  88.7 20.7 %collective-permute-start.15 = (f32[32,256]{1,0:T(8,128)S(1)}, f32[32,256]{1,0:T(8,128)S(1)}, u32[]{:S(2)}, u32[]{:S(2)}) collective-permute-start(f32[32,256]{1,0:T(8,128)S(1)} %fusion.5), channel_id=1, source_target_pairs={{0,12},{4,0},{8,4},{12,8},{16,28},{20,16},{24,20},{28,24},{1,13},{... | collective-permute-start | bytes 98312 | tf_op jit(solution)/shard_map/ppermute | solution.py:227
  100.0 9.5 %collective-permute-start.3 = (f32[520,256]{1,0:T(8,128)S(1)}, f32[520,256]{1,0:T(8,128)S(1)}, u32[]{:S(2)}, u32[]{:S(2)}) collective-permute-start(f32[520,256]{1,0:T(8,128)S(1)} %get-tuple-element.33), channel_id=1, source_target_pairs={{0,4},{4,8},{8,12},{12,0},{16,20},{20,24},{24,28},{28,16},{1,5},{5... | collective-permute-start | bytes 1597448 | tf_op jit(solution)/shard_map/ppermute | solution.py:215
  119.6 16.9 %collective-permute-start.16 = (f32[520,256]{1,0:T(8,128)}, f32[520,256]{1,0:T(8,128)}, u32[]{:S(2)}, u32[]{:S(2)}) collective-permute-start(f32[520,256]{1,0:T(8,128)} %get-tuple-element.22), channel_id=1, source_target_pairs={{0,4},{4,8},{8,12},{12,0},{16,20},{20,24},{24,28},{28,16},{1,5},{5... | collective-permute-start | bytes 1597448 | tf_op jit(solution)/shard_map/ppermute | solution.py:239
  120.8 53.5 %collective-permute-start.19 = (f32[1152,256]{1,0:T(8,128)S(1)}, f32[1152,256]{1,0:T(8,128)S(1)}, u32[]{:S(2)}, u32[]{:S(2)}) collective-permute-start(f32[1152,256]{1,0:T(8,128)S(1)} %get-tuple-element.25), channel_id=1, source_target_pairs={{0,16},{4,20},{8,24},{12,28},{16,0},{20,4},{24,8},{28,12},{1,17},{... | collective-permute-start | bytes 3538952 | tf_op jit(solution)/shard_map/ppermute | solution.py:236
  121.1 36.2 %collective-permute-start.18 = (f32[520,256]{1,0:T(8,128)}, f32[520,256]{1,0:T(8,128)}, u32[]{:S(2)}, u32[]{:S(2)}) collective-permute-start(f32[520,256]{1,0:T(8,128)} %get-tuple-element.24), channel_id=1, source_target_pairs={{0,12},{4,0},{8,4},{12,8},{16,28},{20,16},{24,20},{28,24},{1,13},{... | collective-permute-start | bytes 1597448 | tf_op jit(solution)/shard_map/ppermute | solution.py:239
  122.1 46.6 %collective-permute-start.17 = (f32[520,256]{1,0:T(8,128)}, f32[520,256]{1,0:T(8,128)S(1)}, u32[]{:S(2)}, u32[]{:S(2)}) collective-permute-start(f32[520,256]{1,0:T(8,128)} %get-tuple-element.23), channel_id=1, source_target_pairs={{0,8},{4,12},{8,0},{12,4},{16,24},{20,28},{24,16},{28,20},{1,9},{5... | collective-permute-start | bytes 1597448 | tf_op jit(solution)/shard_map/ppermute | solution.py:239
  (8 other events, 40.5 us)
where the time goes:
time: 181 us
  waiting for transfers between devices  86.2 us (48%)
  starting transfers between devices  29.6 us (16%)
  Pallas kernels  27.1 us (15%)
  between operations  16.5 us (9%)
  local copies, waits for them, and re-layouts  12.5 us (7%)
  other arithmetic  6.66 us (4%)
  matrix products  2.06 us (1%)
    ppermute x3, waiting for transfers between devices, shards(): received.append(lax.ppermute(direct[shift - 1], 'dom', within(shift)))  42.4 us
    pallas_call x1, Pallas kernels, _spmm(): pl.pallas_call(_spmm_kernel, out_shape=jax.ShapeDtypeStruct((dests, out_r...  19.5 us
    ppermute x3, waiting for transfers between devices, shards(): pieces.append(lax.ppermute(projected, 'loop', pairs))  19.4 us
    ppermute x3, waiting for transfers between devices, shards(): held.append(lax.ppermute(own, 'dom', within(shift)))  19.3 us
    ppermute x6, starting transfers between devices, shards(): lax.ppermute((compact[half + shift], jnp.stack([first[shift], second[shif...  10.4 us
    pallas_call x2, Pallas kernels, _combine(): pl.pallas_call(_combine_kernel, out_shape=jax.ShapeDtypeStruct((out_block...  7.6 us
    ppermute x3, starting transfers between devices, shards(): pieces.append(lax.ppermute(projected, 'loop', pairs))  5.94 us
    unnamed x33, local copies, waits for them, and re-layouts  5.41 us
  transfers between devices with their start and end apart: 20, of which 10 were waited for; matrix products, arithmetic and copies ran while one was open for 4% of the time, Pallas kernels for 11%

commit v1 on v0

--- a/solution.py
+++ b/solution.py
@@ -190,15 +190,21 @@
     rotate = order[:, None] == dom_ids[None, :]
     table = jnp.sum(jnp.where(rotate[:, :, None], table[None, :, :], 0), axis=1)
 
+    chunk = width // dom_count
     id_rows = jnp.zeros((dom_count, 8, width), jnp.float32)
-    extra = id_rows.at[:, 0, :CAP].set(table.astype(jnp.float32))
+    id_rows = id_rows.at[:, 0, :CAP].set(table.astype(jnp.float32))
+    extra = jnp.concatenate([jnp.zeros((dom_count, 2 * chunk, width), jnp.float32), id_rows], axis=1)
 
     compact = _spmm(rows, slots, tile_counts, tile_values, partition, extra)
     body_rows = CAP * tile_size
-    chunk = width // dom_count
     chunks = loop_sum.reshape(dom_count, chunk, width)
-    first = [_pick(chunks, order[half + i]) for i in range(half)]
-    second = [_pick(chunks, order[i]) for i in range(half)]
+    first = jnp.stack([_pick(chunks, order[i]) for i in range(dom_count)])
+    second = jnp.concatenate(
+        [jnp.zeros((half, chunk, width), jnp.float32), first[:half]], axis=0
+    )
+    compact = lax.dynamic_update_slice(
+        compact, jnp.concatenate([first, second], axis=1), (0, body_rows, 0)
+    )
 
     def within(shift):
         return [(i, (i // half) * half + (i % half + shift) % half) for i in range(dom_count)]
@@ -206,18 +212,16 @@
     swap = [(i, (1 - i // half) * half + i % half) for i in range(dom_count)]
 
     def ids_of(slabs):
-        return jnp.concatenate([slab[body_rows, :CAP] for slab in slabs]).astype(jnp.int32)
+        return jnp.concatenate([slab[body_rows + 2 * chunk, :CAP] for slab in slabs]).astype(jnp.int32)
 
     relay = [compact[half]]
-    relay_chunk = first[0]
-    own = second[0]
     for shift in range(1, half):
-        slab, pair = lax.ppermute(
-            (compact[half + shift], jnp.stack([first[shift], second[shift]])), "dom", within(shift)
-        )
-        relay.append(slab)
-        relay_chunk = relay_chunk + pair[0]
-        own = own + pair[1]
+        relay.append(lax.ppermute(compact[half + shift], "dom", within(shift)))
+    relay_chunk = relay[0][body_rows:body_rows + chunk]
+    own = relay[0][body_rows + chunk:body_rows + 2 * chunk]
+    for slab in relay[1:]:
+        relay_chunk = relay_chunk + slab[body_rows:body_rows + chunk]
+        own = own + slab[body_rows + chunk:body_rows + 2 * chunk]
     own = own + lax.ppermute(relay_chunk, "dom", swap)
     zeros = jnp.zeros((local_blocks * tile_size, width), jnp.float32)
     payload = _combine(ids_of(relay), relay, zeros, local_blocks, tile_size)

time: 181 us -> 167 us (0.923)
  Pallas kernels: 27.1 us -> 14.5 us
  waiting for transfers between devices: 86.2 us -> 82.5 us
    ppermute x6 -> x3, waiting for transfers between devices: 0.02 us -> 27.2 us  [shards(): relay.append(lax.ppermute(compact[half + shift], 'dom', within(shift)))]
    ppermute x3, waiting for transfers between devices: 19.3 us -> 0.01 us  [shards(): held.append(lax.ppermute(own, 'dom', within(shift)))]
    ppermute x3, waiting for transfers between devices: 19.4 us -> 1.8 us  [shards(): pieces.append(lax.ppermute(projected, 'loop', pairs))]
    pallas_call x1, Pallas kernels: 19.5 us -> 6.7 us  [_spmm(): pl.pallas_call(_spmm_kernel, out_shape=jax.ShapeDtypeStruct((dests, out_r...]
    ppermute x3, waiting for transfers between devices: 0.01 us -> 4.62 us  [shards(): terms.append(lax.ppermute(weight_term, 'loop', pairs))]
    ppermute x3, waiting for transfers between devices: 42.4 us -> 46.7 us  [shards(): received.append(lax.ppermute(direct[shift - 1], 'dom', within(shift)))]
    ppermute x1, waiting for transfers between devices: 4.95 us -> 2.16 us  [shards(): partner = lax.ppermute(payload, 'dom', swap)]
    ppermute x1, starting transfers between devices: 0.3 us -> 2.89 us  [shards(): partner = lax.ppermute(payload, 'dom', swap)]
  transfers between devices with their start and end apart: 20 -> 17, of which waited for: 10 -> 10; matrix products, arithmetic and copies ran while one was open for 4% -> 6% of each run, Pallas kernels for 11% -> 6%
where the time goes in v1:
time: 167 us; the launch traced here: 165 us
  waiting for transfers between devices  82.5 us (49%)
  starting transfers between devices  28.9 us (17%)
  between operations  16.6 us (10%)
  Pallas kernels  14.5 us (9%)
  local copies, waits for them, and re-layouts  12.8 us (8%)
  other arithmetic  6.47 us (4%)
  matrix products  3.07 us (2%)
    ppermute x3, waiting for transfers between devices, shards(): received.append(lax.ppermute(direct[shift - 1], 'dom', within(shift)))  46.7 us
    ppermute x3, waiting for transfers between devices, shards(): relay.append(lax.ppermute(compact[half + shift], 'dom', within(shift)))  27.2 us
    ppermute x3, starting transfers between devices, shards(): relay.append(lax.ppermute(compact[half + shift], 'dom', within(shift)))  11.5 us
    pallas_call x2, Pallas kernels, _combine(): pl.pallas_call(_combine_kernel, out_shape=jax.ShapeDtypeStruct((out_block...  7.77 us
    pallas_call x1, Pallas kernels, _spmm(): pl.pallas_call(_spmm_kernel, out_shape=jax.ShapeDtypeStruct((dests, out_r...  6.7 us
    ppermute x3, starting transfers between devices, shards(): pieces.append(lax.ppermute(projected, 'loop', pairs))  5.94 us
    unnamed x36, local copies, waits for them, and re-layouts  5.08 us
    ppermute x3, waiting for transfers between devices, shards(): terms.append(lax.ppermute(weight_term, 'loop', pairs))  4.62 us
  transfers between devices with their start and end apart: 17, of which 10 were waited for; matrix products, arithmetic and copies ran while one was open for 6% of the time, Pallas kernels for 6%

profile of v1, /device:TPU:0, one launch (start us, length us, event | category | flops | bytes accessed | tf_op | source)
XLA Modules:
  0.0 164.8 jit_solution(12847266300745278325)
XLA Ops:
  0.7 1.6 convolution_convert_fusion
  2.3 3.0 %collective-permute-start = (bf16[1024,256]{1,0:T(8,128)(2,1)S(1)}, bf16[1024,256]{1,0:T(8,128)(2,1)S(1)}, u32[]{:S(2)}, u32[]{:S(2)}) collective-permute-start(bf16[1024,256]{1,0:T(8,128)(2,1)S(1)} %convolution_convert_fusion), channel_id=1, source_target_pairs={{0,1},{1,2},{2,3},{3,0},{4,5},{5,6},{6,7},{7,4},{8,9},{9,10},{10,1... | collective-permute-start | bytes 1572872 | tf_op jit(solution)/shard_map/ppermute | solution.py:148
  5.3 1.5 collective-permute-start.1
  6.8 1.4 collective-permute-start.2
  26.5 1.4 fusion
  27.9 1.5 collective-permute-done.1
  29.9 1.5 collective-permute-start.4
  31.3 1.7 %collective-permute-start.5 = (f32[256,256]{0,1:T(8,128)S(1)}, f32[256,256]{0,1:T(8,128)S(1)}, u32[]{:S(2)}, u32[]{:S(2)}) collective-permute-start(f32[256,256]{0,1:T(8,128)S(1)} %fusion), channel_id=1, source_target_pairs={{0,3},{1,0},{2,1},{3,2},{4,7},{5,4},{6,5},{7,6},{8,11},{9,8},{10,9... | collective-permute-start | bytes 786440 | tf_op jit(solution)/shard_map/ppermute | solution.py:156
  33.4 6.7 %shard_map.95 = f32[8,584,256]{2,1,0:T(8,128)} custom-call(s32[640]{0:T(1024)S(1)} %get-tuple-element.65.rows_ref, s32[640]{0:T(1024)S(1)} %get-tuple-element.66.slots_ref, s32[1]{0:T(128)} %copy.35.cnt_ref, bf16[640,128,128]{2,1,0:T(8,128)(2,1)} %tv_ref.1, bf16[32,128,256]{2,1,0:T(8,128)(2,1)S(1)} %bitcast.84, f32[8,72,256]{2,1,0:T(8,128)S(1)} %pad.37.extra_ref), custom_call_target="tpu_custom_call" | custom-call | flops 5368709120 | bytes 25755648 | tf_op jit(solution)/shard_map/pallas_call | solution.py:60
  40.5 4.1 %collective-permute-done.3 = f32[256,256]{0,1:T(8,128)S(1)} collective-permute-done((f32[256,256]{0,1:T(8,128)S(1)}, f32[256,256]{0,1:T(8,128)S(1)}, u32[]{:S(2)}, u32[]{:S(2)}) %collective-permute-start.3) | collective-permute-done | bytes 262176 | tf_op jit(solution)/shard_map/ppermute | solution.py:156
  46.0 4.2 %slice_bitcast_fusion.7 = (f32[584,256]{1,0:T(8,128)S(1)}, f32[584,256]{1,0:T(8,128)}, f32[584,256]{1,0:T(8,128)}, f32[584,256]{1,0:T(8,128)}, f32[584,256]{1,0:...) fusion(f32[8,584,256]{2,1,0:T(8,128)} %maximum_dynamic-update-slice_fusion), kind=kLoop, calls=%fused_computation.13 | loop fusion | bytes 9568256 | tf_op jit(solution)/shard_map/squeeze | solution.py:241
  50.4 11.3 %collective-permute-start.7 = (f32[584,256]{1,0:T(8,128)}, f32[584,256]{1,0:T(8,128)S(1)}, u32[]{:S(2)}, u32[]{:S(2)}) collective-permute-start(f32[584,256]{1,0:T(8,128)} %get-tuple-element.40), channel_id=1, source_target_pairs={{0,8},{4,12},{8,0},{12,4},{16,24},{20,28},{24,16},{28,20},{1,9},{5... | collective-permute-start | bytes 1794056 | tf_op jit(solution)/shard_map/ppermute | solution.py:219
  61.8 27.1 %collective-permute-done.7.refs_2_ = f32[584,256]{1,0:T(8,128)S(1)} collective-permute-done((f32[584,256]{1,0:T(8,128)}, f32[584,256]{1,0:T(8,128)S(1)}, u32[]{:S(2)}, u32[]{:S(2)}) %collective-permute-start.7) | collective-permute-done | bytes 598048 | tf_op jit(solution)/shard_map/ppermute | solution.py:219
  92.2 3.9 %shard_map.96 = f32[8,128,256]{2,1,0:T(8,128)} custom-call(s32[16]{0:T(128)} %maximum_convert_fusion.map_ref, f32[584,256]{1,0:T(8,128)} %copy-done.2, f32[584,256]{1,0:T(8,128)} %collective-permute-done.6.refs_1_, f32[584,256]{1,0:T(8,128)} %copy-done.5, f32[584,256]{1,0:T(8,128)} %copy-done.4, f32[1024,256]{1,0:T(8,128)} %broadcast_in_dim.83.refs_4_), custom_call_target="tpu_custom_call" | custom-call | flops 524288 | bytes 4194304 | tf_op jit(solution)/shard_map/pallas_call | solution.py:105
  97.0 1.7 %collective-permute-start.12 = (f32[32,256]{1,0:T(8,128)S(1)}, f32[32,256]{1,0:T(8,128)S(1)}, u32[]{:S(2)}, u32[]{:S(2)}) collective-permute-start(f32[32,256]{1,0:T(8,128)S(1)} %fusion.3), channel_id=1, source_target_pairs={{0,12},{4,0},{8,4},{12,8},{16,28},{20,16},{24,20},{28,24},{1,13},{... | collective-permute-start | bytes 98312 | tf_op jit(solution)/shard_map/ppermute | solution.py:231
  98.7 2.3 %constant_dynamic-update-slice_fusion.12 = f32[1152,256]{1,0:T(8,128)} fusion(f32[1024,256]{1,0:T(8,128)} %bitcast.85), kind=kLoop, calls=%fused_computation.40 | loop fusion | bytes 2097152
  103.5 1.1 collective-permute-start.13
  104.6 2.9 %collective-permute-start.16 = (f32[1152,256]{1,0:T(8,128)}, f32[1152,256]{1,0:T(8,128)S(1)}, u32[]{:S(2)}, u32[]{:S(2)}) collective-permute-start(f32[1152,256]{1,0:T(8,128)} %get-tuple-element.25), channel_id=1, source_target_pairs={{0,16},{4,20},{8,24},{12,28},{16,0},{20,4},{24,8},{28,12},{1,17},{... | collective-permute-start | bytes 3538952 | tf_op jit(solution)/shard_map/ppermute | solution.py:240
  107.9 1.7 %collective-permute-start.14 = (f32[584,256]{1,0:T(8,128)}, f32[584,256]{1,0:T(8,128)S(1)}, u32[]{:S(2)}, u32[]{:S(2)}) collective-permute-start(f32[584,256]{1,0:T(8,128)} %get-tuple-element.23), channel_id=1, source_target_pairs={{0,8},{4,12},{8,0},{12,4},{16,24},{20,28},{24,16},{28,20},{1,9},{5... | collective-permute-start | bytes 1794056 | tf_op jit(solution)/shard_map/ppermute | solution.py:243
  109.6 12.5 %collective-permute-done.13.refs_1_ = f32[584,256]{1,0:T(8,128)S(1)} collective-permute-done((f32[584,256]{1,0:T(8,128)}, f32[584,256]{1,0:T(8,128)S(1)}, u32[]{:S(2)}, u32[]{:S(2)}) %collective-permute-start.13) | collective-permute-done | bytes 598048 | tf_op jit(solution)/shard_map/ppermute | solution.py:243
  122.1 25.0 %collective-permute-done.15.refs_3_ = f32[584,256]{1,0:T(8,128)} collective-permute-done((f32[584,256]{1,0:T(8,128)}, f32[584,256]{1,0:T(8,128)}, u32[]{:S(2)}, u32[]{:S(2)}) %collective-permute-start.15) | collective-permute-done | bytes 598048 | tf_op jit(solution)/shard_map/ppermute | solution.py:243
  147.8 9.2 %collective-permute-done.14.refs_2_ = f32[584,256]{1,0:T(8,128)S(1)} collective-permute-done((f32[584,256]{1,0:T(8,128)}, f32[584,256]{1,0:T(8,128)S(1)}, u32[]{:S(2)}, u32[]{:S(2)}) %collective-permute-start.14) | collective-permute-done | bytes 598048 | tf_op jit(solution)/shard_map/ppermute | solution.py:243
  157.7 2.2 %collective-permute-done.16.refs_4_ = f32[1152,256]{1,0:T(8,128)S(1)} collective-permute-done((f32[1152,256]{1,0:T(8,128)}, f32[1152,256]{1,0:T(8,128)S(1)}, u32[]{:S(2)}, u32[]{:S(2)}) %collective-permute-start.16) | collective-permute-done | bytes 1179680 | tf_op jit(solution)/shard_map/ppermute | solution.py:240
  161.0 3.9 %shard_map.97 = f32[8,128,256]{2,1,0:T(8,128)} custom-call(s32[16]{0:T(128)} %maximum_convert_fusion.1.map_ref, f32[584,256]{1,0:T(8,128)} %copy-done.1, f32[584,256]{1,0:T(8,128)} %copy-done.6, f32[584,256]{1,0:T(8,128)} %copy-done.7, f32[584,256]{1,0:T(8,128)} %collective-permute-done.15.refs_3_, f32[1152,256]{1,0:T(8,128)} %copy-done.3), custom_call_target="tpu_custom_call" | custom-call | flops 524288 | bytes 4194304 | tf_op jit(solution)/shard_map/pallas_call | solution.py:105
  (94 shorter events, 14.6 us)
Async XLA Ops:
  0.6 25.8 %copy-start = (bf16[1024,256]{1,0:T(8,128)(2,1)S(1)}, bf16[1024,256]{1,0:T(8,128)(2,1)}, u32[]{:S(2)}) copy-start(bf16[1024,256]{1,0:T(8,128)(2,1)} %param.12) | copy-start | bytes 1572868
  0.6 25.8 %copy-start.9 = (bf16[1024,256]{1,0:T(8,128)(2,1)S(1)}, bf16[1024,256]{1,0:T(8,128)(2,1)}, u32[]{:S(2)}) copy-start(bf16[1024,256]{1,0:T(8,128)(2,1)} %param.10) | copy-start | bytes 1572868
  0.7 20.7 %copy-start.8 = (s32[1,640]{1,0:T(1,128)S(1)}, s32[1,640]{1,0:T(1,128)}, u32[]{:S(2)}) copy-start(s32[1,640]{1,0:T(1,128)} %param.15) | copy-start | bytes 7684
  2.3 25.6 %collective-permute-start = (bf16[1024,256]{1,0:T(8,128)(2,1)S(1)}, bf16[1024,256]{1,0:T(8,128)(2,1)S(1)}, u32[]{:S(2)}, u32[]{:S(2)}) collective-permute-start(bf16[1024,256]{1,0:T(8,128)(2,1)S(1)} %convolution_convert_fusion), channel_id=1, source_target_pairs={{0,1},{1,2},{2,3},{3,0},{4,5},{5,6},{6,7},{7,4},{8,9},{9,10},{10,1... | collective-permute-start | bytes 1572872 | tf_op jit(solution)/shard_map/ppermute | solution.py:148
  5.3 24.1 %collective-permute-start.1 = (bf16[1024,256]{1,0:T(8,128)(2,1)S(1)}, bf16[1024,256]{1,0:T(8,128)(2,1)S(1)}, u32[]{:S(2)}, u32[]{:S(2)}) collective-permute-start(bf16[1024,256]{1,0:T(8,128)(2,1)S(1)} %convolution_convert_fusion), channel_id=1, source_target_pairs={{0,2},{1,3},{2,0},{3,1},{4,6},{5,7},{6,4},{7,5},{8,10},{9,11},{10,... | collective-permute-start | bytes 1572872 | tf_op jit(solution)/shard_map/ppermute | solution.py:148
  6.8 22.9 %collective-permute-start.2 = (bf16[1024,256]{1,0:T(8,128)(2,1)S(1)}, bf16[1024,256]{1,0:T(8,128)(2,1)S(1)}, u32[]{:S(2)}, u32[]{:S(2)}) collective-permute-start(bf16[1024,256]{1,0:T(8,128)(2,1)S(1)} %convolution_convert_fusion), channel_id=1, source_target_pairs={{0,3},{1,0},{2,1},{3,2},{4,7},{5,4},{6,5},{7,6},{8,11},{9,8},{10,9... | collective-permute-start | bytes 1572872 | tf_op jit(solution)/shard_map/ppermute | solution.py:148
  29.9 10.2 %collective-permute-start.4 = (f32[256,256]{0,1:T(8,128)S(1)}, f32[256,256]{0,1:T(8,128)S(1)}, u32[]{:S(2)}, u32[]{:S(2)}) collective-permute-start(f32[256,256]{0,1:T(8,128)S(1)} %fusion), channel_id=1, source_target_pairs={{0,2},{1,3},{2,0},{3,1},{4,6},{5,7},{6,4},{7,5},{8,10},{9,11},{10,... | collective-permute-start | bytes 786440 | tf_op jit(solution)/shard_map/ppermute | solution.py:156
  31.3 9.2 %collective-permute-start.5 = (f32[256,256]{0,1:T(8,128)S(1)}, f32[256,256]{0,1:T(8,128)S(1)}, u32[]{:S(2)}, u32[]{:S(2)}) collective-permute-start(f32[256,256]{0,1:T(8,128)S(1)} %fusion), channel_id=1, source_target_pairs={{0,3},{1,0},{2,1},{3,2},{4,7},{5,4},{6,5},{7,6},{8,11},{9,8},{10,9... | collective-permute-start | bytes 786440 | tf_op jit(solution)/shard_map/ppermute | solution.py:156
  33.1 11.6 %collective-permute-start.3 = (f32[256,256]{0,1:T(8,128)S(1)}, f32[256,256]{0,1:T(8,128)S(1)}, u32[]{:S(2)}, u32[]{:S(2)}) collective-permute-start(f32[256,256]{0,1:T(8,128)S(1)} %fusion), channel_id=1, source_target_pairs={{0,1},{1,2},{2,3},{3,0},{4,5},{5,6},{6,7},{7,4},{8,9},{9,10},{10,1... | collective-permute-start | bytes 786440 | tf_op jit(solution)/shard_map/ppermute | solution.py:156
  50.3 41.9 %copy-start.2 = (f32[584,256]{1,0:T(8,128)}, f32[584,256]{1,0:T(8,128)S(1)}, u32[]{:S(2)}) copy-start(f32[584,256]{1,0:T(8,128)S(1)} %get-tuple-element.42.refs_0_) | copy-start | bytes 1794052
  50.3 59.3 %copy-start.1 = (f32[584,256]{1,0:T(8,128)}, f32[584,256]{1,0:T(8,128)S(1)}, u32[]{:S(2)}) copy-start(f32[584,256]{1,0:T(8,128)S(1)} %get-tuple-element.38.refs_0_) | copy-start | bytes 1794052
  50.3 11.5 %collective-permute-start.8 = (f32[584,256]{1,0:T(8,128)}, f32[584,256]{1,0:T(8,128)S(1)}, u32[]{:S(2)}, u32[]{:S(2)}) collective-permute-start(f32[584,256]{1,0:T(8,128)} %get-tuple-element.39), channel_id=1, source_target_pairs={{0,12},{4,0},{8,4},{12,8},{16,28},{20,16},{24,20},{28,24},{1,13},{... | collective-permute-start | bytes 1794056 | tf_op jit(solution)/shard_map/ppermute | solution.py:219
  50.4 38.6 %collective-permute-start.7 = (f32[584,256]{1,0:T(8,128)}, f32[584,256]{1,0:T(8,128)S(1)}, u32[]{:S(2)}, u32[]{:S(2)}) collective-permute-start(f32[584,256]{1,0:T(8,128)} %get-tuple-element.40), channel_id=1, source_target_pairs={{0,8},{4,12},{8,0},{12,4},{16,24},{20,28},{24,16},{28,20},{1,9},{5... | collective-permute-start | bytes 1794056 | tf_op jit(solution)/shard_map/ppermute | solution.py:219
  61.7 27.2 %collective-permute-start.6 = (f32[584,256]{1,0:T(8,128)}, f32[584,256]{1,0:T(8,128)}, u32[]{:S(2)}, u32[]{:S(2)}) collective-permute-start(f32[584,256]{1,0:T(8,128)} %get-tuple-element.41), channel_id=1, source_target_pairs={{0,4},{4,8},{8,12},{12,0},{16,20},{20,24},{24,28},{28,16},{1,5},{5... | collective-permute-start | bytes 1794056 | tf_op jit(solution)/shard_map/ppermute | solution.py:219
  61.8 30.4 %copy-start.4 = (f32[584,256]{1,0:T(8,128)}, f32[584,256]{1,0:T(8,128)S(1)}, u32[]{:S(2)}) copy-start(f32[584,256]{1,0:T(8,128)S(1)} %collective-permute-done.8.refs_3_) | copy-start | bytes 1794052
  89.8 6.3 %collective-permute-start.9 = (f32[32,256]{1,0:T(8,128)S(1)}, f32[32,256]{1,0:T(8,128)S(1)}, u32[]{:S(2)}, u32[]{:S(2)}) collective-permute-start(f32[32,256]{1,0:T(8,128)S(1)} %slice_add_fusion), channel_id=1, source_target_pairs={{0,16},{4,20},{8,24},{12,28},{16,0},{20,4},{24,8},{28,12},{1,17},{... | collective-permute-start | bytes 98312 | tf_op jit(solution)/shard_map/ppermute | solution.py:225
  96.9 4.1 %collective-permute-start.10 = (f32[32,256]{1,0:T(8,128)S(1)}, f32[32,256]{1,0:T(8,128)S(1)}, u32[]{:S(2)}, u32[]{:S(2)}) collective-permute-start(f32[32,256]{1,0:T(8,128)S(1)} %fusion.3), channel_id=1, source_target_pairs={{0,4},{4,8},{8,12},{12,0},{16,20},{20,24},{24,28},{28,16},{1,5},{5... | collective-permute-start | bytes 98312 | tf_op jit(solution)/shard_map/ppermute | solution.py:231
  96.9 4.0 %collective-permute-start.11 = (f32[32,256]{1,0:T(8,128)S(1)}, f32[32,256]{1,0:T(8,128)S(1)}, u32[]{:S(2)}, u32[]{:S(2)}) collective-permute-start(f32[32,256]{1,0:T(8,128)S(1)} %fusion.3), channel_id=1, source_target_pairs={{0,8},{4,12},{8,0},{12,4},{16,24},{20,28},{24,16},{28,20},{1,9},{5... | collective-permute-start | bytes 98312 | tf_op jit(solution)/shard_map/ppermute | solution.py:231
  97.0 4.0 %collective-permute-start.12 = (f32[32,256]{1,0:T(8,128)S(1)}, f32[32,256]{1,0:T(8,128)S(1)}, u32[]{:S(2)}, u32[]{:S(2)}) collective-permute-start(f32[32,256]{1,0:T(8,128)S(1)} %fusion.3), channel_id=1, source_target_pairs={{0,12},{4,0},{8,4},{12,8},{16,28},{20,16},{24,20},{28,24},{1,13},{... | collective-permute-start | bytes 98312 | tf_op jit(solution)/shard_map/ppermute | solution.py:231
  103.5 18.6 %collective-permute-start.13 = (f32[584,256]{1,0:T(8,128)}, f32[584,256]{1,0:T(8,128)S(1)}, u32[]{:S(2)}, u32[]{:S(2)}) collective-permute-start(f32[584,256]{1,0:T(8,128)} %get-tuple-element.22), channel_id=1, source_target_pairs={{0,4},{4,8},{8,12},{12,0},{16,20},{20,24},{24,28},{28,16},{1,5},{5... | collective-permute-start | bytes 1794056 | tf_op jit(solution)/shard_map/ppermute | solution.py:243
  104.6 55.2 %collective-permute-start.16 = (f32[1152,256]{1,0:T(8,128)}, f32[1152,256]{1,0:T(8,128)S(1)}, u32[]{:S(2)}, u32[]{:S(2)}) collective-permute-start(f32[1152,256]{1,0:T(8,128)} %get-tuple-element.25), channel_id=1, source_target_pairs={{0,16},{4,20},{8,24},{12,28},{16,0},{20,4},{24,8},{28,12},{1,17},{... | collective-permute-start | bytes 3538952 | tf_op jit(solution)/shard_map/ppermute | solution.py:240
  107.5 39.6 %collective-permute-start.15 = (f32[584,256]{1,0:T(8,128)}, f32[584,256]{1,0:T(8,128)}, u32[]{:S(2)}, u32[]{:S(2)}) collective-permute-start(f32[584,256]{1,0:T(8,128)} %get-tuple-element.24), channel_id=1, source_target_pairs={{0,12},{4,0},{8,4},{12,8},{16,28},{20,16},{24,20},{28,24},{1,13},{... | collective-permute-start | bytes 1794056 | tf_op jit(solution)/shard_map/ppermute | solution.py:243
  107.9 49.1 %collective-permute-start.14 = (f32[584,256]{1,0:T(8,128)}, f32[584,256]{1,0:T(8,128)S(1)}, u32[]{:S(2)}, u32[]{:S(2)}) collective-permute-start(f32[584,256]{1,0:T(8,128)} %get-tuple-element.23), channel_id=1, source_target_pairs={{0,8},{4,12},{8,0},{12,4},{16,24},{20,28},{24,16},{28,20},{1,9},{5... | collective-permute-start | bytes 1794056 | tf_op jit(solution)/shard_map/ppermute | solution.py:243
  122.1 38.7 %copy-start.6 = (f32[584,256]{1,0:T(8,128)}, f32[584,256]{1,0:T(8,128)S(1)}, u32[]{:S(2)}) copy-start(f32[584,256]{1,0:T(8,128)S(1)} %collective-permute-done.13.refs_1_) | copy-start | bytes 1794052
  (3 other events, 7.3 us)

commit v2 on v1

--- a/solution.py
+++ b/solution.py
@@ -193,7 +193,7 @@
     chunk = width // dom_count
     id_rows = jnp.zeros((dom_count, 8, width), jnp.float32)
     id_rows = id_rows.at[:, 0, :CAP].set(table.astype(jnp.float32))
-    extra = jnp.concatenate([jnp.zeros((dom_count, 2 * chunk, width), jnp.float32), id_rows], axis=1)
+    extra = jnp.concatenate([id_rows, jnp.zeros((dom_count, 2 * chunk, width), jnp.float32)], axis=1)
 
     compact = _spmm(rows, slots, tile_counts, tile_values, partition, extra)
     body_rows = CAP * tile_size
@@ -203,7 +203,7 @@
         [jnp.zeros((half, chunk, width), jnp.float32), first[:half]], axis=0
     )
     compact = lax.dynamic_update_slice(
-        compact, jnp.concatenate([first, second], axis=1), (0, body_rows, 0)
+        compact, jnp.concatenate([first, second], axis=1), (0, body_rows + 8, 0)
     )
 
     def within(shift):
@@ -212,16 +212,17 @@
     swap = [(i, (1 - i // half) * half + i % half) for i in range(dom_count)]
 
     def ids_of(slabs):
-        return jnp.concatenate([slab[body_rows + 2 * chunk, :CAP] for slab in slabs]).astype(jnp.int32)
+        return jnp.concatenate([slab[body_rows, :CAP] for slab in slabs]).astype(jnp.int32)
 
     relay = [compact[half]]
     for shift in range(1, half):
         relay.append(lax.ppermute(compact[half + shift], "dom", within(shift)))
-    relay_chunk = relay[0][body_rows:body_rows + chunk]
-    own = relay[0][body_rows + chunk:body_rows + 2 * chunk]
+    lead = body_rows + 8
+    relay_chunk = relay[0][lead:lead + chunk]
+    own = relay[0][lead + chunk:lead + 2 * chunk]
     for slab in relay[1:]:
-        relay_chunk = relay_chunk + slab[body_rows:body_rows + chunk]
-        own = own + slab[body_rows + chunk:body_rows + 2 * chunk]
+        relay_chunk = relay_chunk + slab[lead:lead + chunk]
+        own = own + slab[lead + chunk:lead + 2 * chunk]
     own = own + lax.ppermute(relay_chunk, "dom", swap)
     zeros = jnp.zeros((local_blocks * tile_size, width), jnp.float32)
     payload = _combine(ids_of(relay), relay, zeros, local_blocks, tile_size)
@@ -235,12 +236,12 @@
     )
     payload = jnp.concatenate([payload.reshape(node_rows, width), half_chunks], axis=0)
 
-    direct = [compact[shift] for shift in range(1, half)]
-    direct, payload = lax.optimization_barrier((direct, payload))
-    partner = lax.ppermute(payload, "dom", swap)
-    received = [compact[0]]
+    direct = [compact[shift, :body_rows + 8] for shift in range(1, half)]
+    direct, relay = lax.optimization_barrier((direct, relay))
+    received = [compact[0, :body_rows + 8]]
     for shift in range(1, half):
         received.append(lax.ppermute(direct[shift - 1], "dom", within(shift)))
+    partner = lax.ppermute(payload, "dom", swap)
     node_grad = _combine(ids_of(received), received, partner, local_blocks, tile_size)
     node_grad = node_grad.reshape(node_rows, width)
     other_chunks = partner[node_rows:]

time: 167 us -> 165 us (0.988)
  waiting for transfers between devices: 82.5 us -> 76.2 us
  Pallas kernels: 14.5 us -> 18.5 us
    ppermute x1, waiting for transfers between devices: 2.16 us -> 13 us  [shards(): partner = lax.ppermute(payload, 'dom', swap)]
    ppermute x3, waiting for transfers between devices: 46.7 us -> 36.1 us  [shards(): received.append(lax.ppermute(direct[shift - 1], 'dom', within(shift)))]
    ppermute x3, waiting for transfers between devices: 27.2 us -> 22.2 us  [shards(): relay.append(lax.ppermute(compact[half + shift], 'dom', within(shift)))]
    ppermute x3, waiting for transfers between devices: 4.62 us -> 0.05 us  [shards(): terms.append(lax.ppermute(weight_term, 'loop', pairs))]
    pallas_call x1, Pallas kernels: 6.7 us -> 10.8 us  [_spmm(): pl.pallas_call(_spmm_kernel, out_shape=jax.ShapeDtypeStruct((dests, out_r...]
    ppermute x3, waiting for transfers between devices: 1.8 us -> 3.69 us  [shards(): pieces.append(lax.ppermute(projected, 'loop', pairs))]
    squeeze x9 -> x10, local copies, waits for them, and re-layouts: 5.58 us -> 7.01 us  [the longest x1 2.87 us: shards(): relay.append(lax.ppermute(compact[half + shift], 'dom', within(shift)))]
    unnamed x36 -> x34, local copies, waits for them, and re-layouts: 5.08 us -> 5.08 us
  transfers between devices with their start and end apart: 17 -> 17, of which waited for: 10 -> 7; matrix products, arithmetic and copies ran while one was open for 6% -> 10% of each run, Pallas kernels for 6% -> 9%
where the time goes in v2:
time: 165 us; the launch traced here: 163 us
  waiting for transfers between devices  76.2 us (46%)
  starting transfers between devices  27.4 us (17%)
  Pallas kernels  18.5 us (11%)
  between operations  16.6 us (10%)
  local copies, waits for them, and re-layouts  14.2 us (9%)
  other arithmetic  6.6 us (4%)
  matrix products  3.19 us (2%)
    ppermute x3, waiting for transfers between devices, shards(): received.append(lax.ppermute(direct[shift - 1], 'dom', within(shift)))  36.1 us
    ppermute x3, waiting for transfers between devices, shards(): relay.append(lax.ppermute(compact[half + shift], 'dom', within(shift)))  22.2 us
    ppermute x1, waiting for transfers between devices, shards(): partner = lax.ppermute(payload, 'dom', swap)  13 us
    ppermute x3, starting transfers between devices, shards(): relay.append(lax.ppermute(compact[half + shift], 'dom', within(shift)))  12.1 us
    pallas_call x1, Pallas kernels, _spmm(): pl.pallas_call(_spmm_kernel, out_shape=jax.ShapeDtypeStruct((dests, out_r...  10.8 us
    pallas_call x2, Pallas kernels, _combine(): pl.pallas_call(_combine_kernel, out_shape=jax.ShapeDtypeStruct((out_block...  7.7 us
    unnamed x34, local copies, waits for them, and re-layouts  5.08 us
    ppermute x3, starting transfers between devices, shards(): pieces.append(lax.ppermute(projected, 'loop', pairs))  5.04 us
  transfers between devices with their start and end apart: 17, of which 7 were waited for; matrix products, arithmetic and copies ran while one was open for 10% of the time, Pallas kernels for 9%

profile of v2, /device:TPU:0, one launch (start us, length us, event | category | flops | bytes accessed | tf_op | source)
XLA Modules:
  0.0 162.8 jit_solution(14609931488279896588)
XLA Ops:
  0.7 1.6 convolution_convert_fusion
  2.3 4.0 %collective-permute-start.2 = (bf16[1024,256]{1,0:T(8,128)(2,1)S(1)}, bf16[1024,256]{1,0:T(8,128)(2,1)S(1)}, u32[]{:S(2)}, u32[]{:S(2)}) collective-permute-start(bf16[1024,256]{1,0:T(8,128)(2,1)S(1)} %convolution_convert_fusion), channel_id=1, source_target_pairs={{0,3},{1,0},{2,1},{3,2},{4,7},{5,4},{6,5},{7,6},{8,11},{9,8},{10,9... | collective-permute-start | bytes 1572872 | tf_op jit(solution)/shard_map/ppermute | solution.py:148
  25.5 1.6 fusion
  27.1 3.7 %collective-permute-done.1 = bf16[1024,256]{1,0:T(8,128)(2,1)S(1)} collective-permute-done((bf16[1024,256]{1,0:T(8,128)(2,1)S(1)}, bf16[1024,256]{1,0:T(8,128)(2,1)S(1)}, u32[]{:S(2)}, u32[]{:S(2)}) %collective-permute-start.1) | collective-permute-done | bytes 524320 | tf_op jit(solution)/shard_map/ppermute | solution.py:148
  31.6 1.2 collective-permute-start.4
  33.6 10.8 %shard_map.95 = f32[8,584,256]{2,1,0:T(8,128)} custom-call(s32[640]{0:T(1024)S(1)} %get-tuple-element.63.rows_ref, s32[640]{0:T(1024)S(1)} %get-tuple-element.64.slots_ref, s32[1]{0:T(128)} %copy.35.cnt_ref, bf16[640,128,128]{2,1,0:T(8,128)(2,1)} %tv_ref.1, bf16[32,128,256]{2,1,0:T(8,128)(2,1)S(1)} %bitcast.84, f32[8,72,256]{2,1,0:T(8,128)S(1)} %pad.37.extra_ref), custom_call_target="tpu_custom_call" | custom-call | flops 5368709120 | bytes 25755648 | tf_op jit(solution)/shard_map/pallas_call | solution.py:60
  45.8 2.9 %slice_bitcast_fusion = (f32[584,256]{1,0:T(8,128)}, f32[584,256]{1,0:T(8,128)}, f32[584,256]{1,0:T(8,128)}, f32[584,256]{1,0:T(8,128)S(1)}) fusion(f32[8,584,256]{2,1,0:T(8,128)} %maximum_dynamic-update-slice_fusion), kind=kLoop, calls=%fused_computation.6 | loop fusion | bytes 4784128 | tf_op jit(solution)/shard_map/squeeze | solution.py:219
  48.7 10.7 %collective-permute-start.7 = (f32[584,256]{1,0:T(8,128)}, f32[584,256]{1,0:T(8,128)S(1)}, u32[]{:S(2)}, u32[]{:S(2)}) collective-permute-start(f32[584,256]{1,0:T(8,128)} %get-tuple-element.41), channel_id=1, source_target_pairs={{0,8},{4,12},{8,0},{12,4},{16,24},{20,28},{24,16},{28,20},{1,9},{5... | collective-permute-start | bytes 1794056 | tf_op jit(solution)/shard_map/ppermute | solution.py:219
  59.4 1.4 collective-permute-start.8
  60.8 2.8 %slice_bitcast_fusion.7 = (f32[520,256]{1,0:T(8,128)S(1)}, f32[520,256]{1,0:T(8,128)}, f32[520,256]{1,0:T(8,128)}, f32[520,256]{1,0:T(8,128)}) fusion(f32[8,584,256]{2,1,0:T(8,128)} %maximum_dynamic-update-slice_fusion), kind=kLoop, calls=%fused_computation.13 | loop fusion | bytes 4259840 | tf_op jit(solution)/shard_map/squeeze | solution.py:241
  63.6 9.9 %collective-permute-done.7.refs_2_ = f32[584,256]{1,0:T(8,128)S(1)} collective-permute-done((f32[584,256]{1,0:T(8,128)}, f32[584,256]{1,0:T(8,128)S(1)}, u32[]{:S(2)}, u32[]{:S(2)}) %collective-permute-start.7) | collective-permute-done | bytes 598048 | tf_op jit(solution)/shard_map/ppermute | solution.py:219
  73.5 12.3 %collective-permute-done.8.refs_3_ = f32[584,256]{1,0:T(8,128)} collective-permute-done((f32[584,256]{1,0:T(8,128)}, f32[584,256]{1,0:T(8,128)}, u32[]{:S(2)}, u32[]{:S(2)}) %collective-permute-start.8) | collective-permute-done | bytes 598048 | tf_op jit(solution)/shard_map/ppermute | solution.py:219
  85.8 1.9 %collective-permute-start.11 = (f32[520,256]{1,0:T(8,128)}, f32[520,256]{1,0:T(8,128)}, u32[]{:S(2)}, u32[]{:S(2)}) collective-permute-start(f32[520,256]{1,0:T(8,128)} %get-tuple-element.23), channel_id=1, source_target_pairs={{0,12},{4,0},{8,4},{12,8},{16,28},{20,16},{24,20},{28,24},{1,13},{... | collective-permute-start | bytes 1597448 | tf_op jit(solution)/shard_map/ppermute | solution.py:243
  89.8 1.0 broadcast_in_dim.83.refs_4_
  90.9 3.9 %shard_map.96 = f32[8,128,256]{2,1,0:T(8,128)} custom-call(s32[16]{0:T(128)} %maximum_convert_fusion.1.map_ref, f32[584,256]{1,0:T(8,128)} %copy-done.1, f32[584,256]{1,0:T(8,128)} %copy-done.4, f32[584,256]{1,0:T(8,128)} %copy-done.5, f32[584,256]{1,0:T(8,128)} %collective-permute-done.8.refs_3_, f32[1024,256]{1,0:T(8,128)} %broadcast_in_dim.83.refs_4_), custom_call_target="tpu_custom_call" | custom-call | flops 524288 | bytes 4194304 | tf_op jit(solution)/shard_map/pallas_call | solution.py:105
  95.9 2.1 %collective-permute-start.14 = (f32[32,256]{1,0:T(8,128)S(1)}, f32[32,256]{1,0:T(8,128)S(1)}, u32[]{:S(2)}, u32[]{:S(2)}) collective-permute-start(f32[32,256]{1,0:T(8,128)S(1)} %fusion.3), channel_id=1, source_target_pairs={{0,8},{4,12},{8,0},{12,4},{16,24},{20,28},{24,16},{28,20},{1,9},{5... | collective-permute-start | bytes 98312 | tf_op jit(solution)/shard_map/ppermute | solution.py:232
  98.1 2.3 %constant_dynamic-update-slice_fusion.12 = f32[1152,256]{1,0:T(8,128)} fusion(f32[1024,256]{1,0:T(8,128)} %bitcast.85), kind=kLoop, calls=%fused_computation.40 | loop fusion | bytes 2097152
  100.4 0.9 collective-permute-done.13
  103.8 2.1 %collective-permute-start.16 = (f32[1152,256]{1,0:T(8,128)}, f32[1152,256]{1,0:T(8,128)S(1)}, u32[]{:S(2)}, u32[]{:S(2)}) collective-permute-start(f32[1152,256]{1,0:T(8,128)} %get-tuple-element.47), channel_id=1, source_target_pairs={{0,16},{4,20},{8,24},{12,28},{16,0},{20,4},{24,8},{28,12},{1,17},{... | collective-permute-start | bytes 3538952 | tf_op jit(solution)/shard_map/ppermute | solution.py:244
  105.9 1.3 collective-permute-start.10
  107.9 36.1 %collective-permute-done.10.refs_2_ = f32[520,256]{1,0:T(8,128)S(1)} collective-permute-done((f32[520,256]{1,0:T(8,128)}, f32[520,256]{1,0:T(8,128)S(1)}, u32[]{:S(2)}, u32[]{:S(2)}) %collective-permute-start.10) | collective-permute-done | bytes 532512 | tf_op jit(solution)/shard_map/ppermute | solution.py:243
  144.9 13.0 %collective-permute-done.16.refs_4_ = f32[1152,256]{1,0:T(8,128)S(1)} collective-permute-done((f32[1152,256]{1,0:T(8,128)}, f32[1152,256]{1,0:T(8,128)S(1)}, u32[]{:S(2)}, u32[]{:S(2)}) %collective-permute-start.16) | collective-permute-done | bytes 1179680 | tf_op jit(solution)/shard_map/ppermute | solution.py:244
  158.0 0.9 broadcast_select_fusion
  159.0 3.8 %shard_map.97 = f32[8,128,256]{2,1,0:T(8,128)} custom-call(s32[16]{0:T(128)} %maximum_convert_fusion.map_ref, f32[520,256]{1,0:T(8,128)} %copy-done.2, f32[520,256]{1,0:T(8,128)} %copy-done.7, f32[520,256]{1,0:T(8,128)} %copy-done.6, f32[520,256]{1,0:T(8,128)} %collective-permute-done.11.refs_3_, f32[1152,256]{1,0:T(8,128)} %copy-done.3), custom_call_target="tpu_custom_call" | custom-call | flops 524288 | bytes 4194304 | tf_op jit(solution)/shard_map/pallas_call | solution.py:105
  (93 shorter events, 14.1 us)
Async XLA Ops:
  0.6 24.9 %copy-start = (bf16[1024,256]{1,0:T(8,128)(2,1)S(1)}, bf16[1024,256]{1,0:T(8,128)(2,1)}, u32[]{:S(2)}) copy-start(bf16[1024,256]{1,0:T(8,128)(2,1)} %param.12) | copy-start | bytes 1572868
  0.6 19.7 %copy-start.8 = (s32[1,640]{1,0:T(1,128)S(1)}, s32[1,640]{1,0:T(1,128)}, u32[]{:S(2)}) copy-start(s32[1,640]{1,0:T(1,128)} %param.15) | copy-start | bytes 7684
  2.3 24.9 %collective-permute-start.2 = (bf16[1024,256]{1,0:T(8,128)(2,1)S(1)}, bf16[1024,256]{1,0:T(8,128)(2,1)S(1)}, u32[]{:S(2)}, u32[]{:S(2)}) collective-permute-start(bf16[1024,256]{1,0:T(8,128)(2,1)S(1)} %convolution_convert_fusion), channel_id=1, source_target_pairs={{0,3},{1,0},{2,1},{3,2},{4,7},{5,4},{6,5},{7,6},{8,11},{9,8},{10,9... | collective-permute-start | bytes 1572872 | tf_op jit(solution)/shard_map/ppermute | solution.py:148
  6.2 24.6 %collective-permute-start.1 = (bf16[1024,256]{1,0:T(8,128)(2,1)S(1)}, bf16[1024,256]{1,0:T(8,128)(2,1)S(1)}, u32[]{:S(2)}, u32[]{:S(2)}) collective-permute-start(bf16[1024,256]{1,0:T(8,128)(2,1)S(1)} %convolution_convert_fusion), channel_id=1, source_target_pairs={{0,2},{1,3},{2,0},{3,1},{4,6},{5,7},{6,4},{7,5},{8,10},{9,11},{10,... | collective-permute-start | bytes 1572872 | tf_op jit(solution)/shard_map/ppermute | solution.py:148
  6.7 24.1 %collective-permute-start = (bf16[1024,256]{1,0:T(8,128)(2,1)S(1)}, bf16[1024,256]{1,0:T(8,128)(2,1)S(1)}, u32[]{:S(2)}, u32[]{:S(2)}) collective-permute-start(bf16[1024,256]{1,0:T(8,128)(2,1)S(1)} %convolution_convert_fusion), channel_id=1, source_target_pairs={{0,1},{1,2},{2,3},{3,0},{4,5},{5,6},{6,7},{7,4},{8,9},{9,10},{10,1... | collective-permute-start | bytes 1572872 | tf_op jit(solution)/shard_map/ppermute | solution.py:148
  31.0 13.4 %collective-permute-start.5 = (f32[256,256]{0,1:T(8,128)S(1)}, f32[256,256]{0,1:T(8,128)S(1)}, u32[]{:S(2)}, u32[]{:S(2)}) collective-permute-start(f32[256,256]{0,1:T(8,128)S(1)} %fusion), channel_id=1, source_target_pairs={{0,3},{1,0},{2,1},{3,2},{4,7},{5,4},{6,5},{7,6},{8,11},{9,8},{10,9... | collective-permute-start | bytes 786440 | tf_op jit(solution)/shard_map/ppermute | solution.py:156
  31.6 12.9 %collective-permute-start.4 = (f32[256,256]{0,1:T(8,128)S(1)}, f32[256,256]{0,1:T(8,128)S(1)}, u32[]{:S(2)}, u32[]{:S(2)}) collective-permute-start(f32[256,256]{0,1:T(8,128)S(1)} %fusion), channel_id=1, source_target_pairs={{0,2},{1,3},{2,0},{3,1},{4,6},{5,7},{6,4},{7,5},{8,10},{9,11},{10,... | collective-permute-start | bytes 786440 | tf_op jit(solution)/shard_map/ppermute | solution.py:156
  32.8 11.6 %collective-permute-start.3 = (f32[256,256]{0,1:T(8,128)S(1)}, f32[256,256]{0,1:T(8,128)S(1)}, u32[]{:S(2)}, u32[]{:S(2)}) collective-permute-start(f32[256,256]{0,1:T(8,128)S(1)} %fusion), channel_id=1, source_target_pairs={{0,1},{1,2},{2,3},{3,0},{4,5},{5,6},{6,7},{7,4},{8,9},{9,10},{10,1... | collective-permute-start | bytes 786440 | tf_op jit(solution)/shard_map/ppermute | solution.py:156
  48.7 14.9 %copy-start.1 = (f32[584,256]{1,0:T(8,128)}, f32[584,256]{1,0:T(8,128)S(1)}, u32[]{:S(2)}) copy-start(f32[584,256]{1,0:T(8,128)S(1)} %get-tuple-element.43.refs_0_) | copy-start | bytes 1794052
  48.7 14.9 %collective-permute-start.6 = (f32[584,256]{1,0:T(8,128)}, f32[584,256]{1,0:T(8,128)S(1)}, u32[]{:S(2)}, u32[]{:S(2)}) collective-permute-start(f32[584,256]{1,0:T(8,128)} %get-tuple-element.42), channel_id=1, source_target_pairs={{0,4},{4,8},{8,12},{12,0},{16,20},{20,24},{24,28},{28,16},{1,5},{5... | collective-permute-start | bytes 1794056 | tf_op jit(solution)/shard_map/ppermute | solution.py:219
  48.7 24.9 %collective-permute-start.7 = (f32[584,256]{1,0:T(8,128)}, f32[584,256]{1,0:T(8,128)S(1)}, u32[]{:S(2)}, u32[]{:S(2)}) collective-permute-start(f32[584,256]{1,0:T(8,128)} %get-tuple-element.41), channel_id=1, source_target_pairs={{0,8},{4,12},{8,0},{12,4},{16,24},{20,28},{24,16},{28,20},{1,9},{5... | collective-permute-start | bytes 1794056 | tf_op jit(solution)/shard_map/ppermute | solution.py:219
  59.4 26.4 %collective-permute-start.8 = (f32[584,256]{1,0:T(8,128)}, f32[584,256]{1,0:T(8,128)}, u32[]{:S(2)}, u32[]{:S(2)}) collective-permute-start(f32[584,256]{1,0:T(8,128)} %get-tuple-element.40), channel_id=1, source_target_pairs={{0,12},{4,0},{8,4},{12,8},{16,28},{20,16},{24,20},{28,24},{1,13},{... | collective-permute-start | bytes 1794056 | tf_op jit(solution)/shard_map/ppermute | solution.py:219
  63.6 43.6 %copy-start.2 = (f32[520,256]{1,0:T(8,128)}, f32[520,256]{1,0:T(8,128)S(1)}, u32[]{:S(2)}) copy-start(f32[520,256]{1,0:T(8,128)S(1)} %get-tuple-element.36.refs_0_) | copy-start | bytes 1597444
  63.6 27.3 %copy-start.4 = (f32[584,256]{1,0:T(8,128)}, f32[584,256]{1,0:T(8,128)S(1)}, u32[]{:S(2)}) copy-start(f32[584,256]{1,0:T(8,128)S(1)} %collective-permute-done.6.refs_1_) | copy-start | bytes 1794052
  73.5 17.3 %copy-start.5 = (f32[584,256]{1,0:T(8,128)}, f32[584,256]{1,0:T(8,128)S(1)}, u32[]{:S(2)}) copy-start(f32[584,256]{1,0:T(8,128)S(1)} %collective-permute-done.7.refs_2_) | copy-start | bytes 1794052
  85.8 21.4 %collective-permute-start.11 = (f32[520,256]{1,0:T(8,128)}, f32[520,256]{1,0:T(8,128)}, u32[]{:S(2)}, u32[]{:S(2)}) collective-permute-start(f32[520,256]{1,0:T(8,128)} %get-tuple-element.23), channel_id=1, source_target_pairs={{0,12},{4,0},{8,4},{12,8},{16,28},{20,16},{24,20},{28,24},{1,13},{... | collective-permute-start | bytes 1597448 | tf_op jit(solution)/shard_map/ppermute | solution.py:243
  88.5 6.6 %collective-permute-start.12 = (f32[32,256]{1,0:T(8,128)S(1)}, f32[32,256]{1,0:T(8,128)S(1)}, u32[]{:S(2)}, u32[]{:S(2)}) collective-permute-start(f32[32,256]{1,0:T(8,128)S(1)} %slice_add_fusion), channel_id=1, source_target_pairs={{0,16},{4,20},{8,24},{12,28},{16,0},{20,4},{24,8},{28,12},{1,17},{... | collective-permute-start | bytes 98312 | tf_op jit(solution)/shard_map/ppermute | solution.py:226
  95.8 4.6 %collective-permute-start.15 = (f32[32,256]{1,0:T(8,128)S(1)}, f32[32,256]{1,0:T(8,128)S(1)}, u32[]{:S(2)}, u32[]{:S(2)}) collective-permute-start(f32[32,256]{1,0:T(8,128)S(1)} %fusion.3), channel_id=1, source_target_pairs={{0,12},{4,0},{8,4},{12,8},{16,28},{20,16},{24,20},{28,24},{1,13},{... | collective-permute-start | bytes 98312 | tf_op jit(solution)/shard_map/ppermute | solution.py:232
  95.9 4.5 %collective-permute-start.14 = (f32[32,256]{1,0:T(8,128)S(1)}, f32[32,256]{1,0:T(8,128)S(1)}, u32[]{:S(2)}, u32[]{:S(2)}) collective-permute-start(f32[32,256]{1,0:T(8,128)S(1)} %fusion.3), channel_id=1, source_target_pairs={{0,8},{4,12},{8,0},{12,4},{16,24},{20,28},{24,16},{28,20},{1,9},{5... | collective-permute-start | bytes 98312 | tf_op jit(solution)/shard_map/ppermute | solution.py:232
  98.0 3.3 %collective-permute-start.13 = (f32[32,256]{1,0:T(8,128)S(1)}, f32[32,256]{1,0:T(8,128)S(1)}, u32[]{:S(2)}, u32[]{:S(2)}) collective-permute-start(f32[32,256]{1,0:T(8,128)S(1)} %fusion.3), channel_id=1, source_target_pairs={{0,4},{4,8},{8,12},{12,0},{16,20},{20,24},{24,28},{28,16},{1,5},{5... | collective-permute-start | bytes 98312 | tf_op jit(solution)/shard_map/ppermute | solution.py:232
  103.8 54.1 %collective-permute-start.16 = (f32[1152,256]{1,0:T(8,128)}, f32[1152,256]{1,0:T(8,128)S(1)}, u32[]{:S(2)}, u32[]{:S(2)}) collective-permute-start(f32[1152,256]{1,0:T(8,128)} %get-tuple-element.47), channel_id=1, source_target_pairs={{0,16},{4,20},{8,24},{12,28},{16,0},{20,4},{24,8},{28,12},{1,17},{... | collective-permute-start | bytes 3538952 | tf_op jit(solution)/shard_map/ppermute | solution.py:244
  105.9 38.1 %collective-permute-start.10 = (f32[520,256]{1,0:T(8,128)}, f32[520,256]{1,0:T(8,128)S(1)}, u32[]{:S(2)}, u32[]{:S(2)}) collective-permute-start(f32[520,256]{1,0:T(8,128)} %get-tuple-element.22), channel_id=1, source_target_pairs={{0,8},{4,12},{8,0},{12,4},{16,24},{20,28},{24,16},{28,20},{1,9},{5... | collective-permute-start | bytes 1597448 | tf_op jit(solution)/shard_map/ppermute | solution.py:243
  107.2 36.8 %collective-permute-start.9 = (f32[520,256]{1,0:T(8,128)}, f32[520,256]{1,0:T(8,128)S(1)}, u32[]{:S(2)}, u32[]{:S(2)}) collective-permute-start(f32[520,256]{1,0:T(8,128)} %get-tuple-element.21), channel_id=1, source_target_pairs={{0,4},{4,8},{8,12},{12,0},{16,20},{20,24},{24,28},{28,16},{1,5},{5... | collective-permute-start | bytes 1597448 | tf_op jit(solution)/shard_map/ppermute | solution.py:243
  144.0 14.9 %copy-start.6 = (f32[520,256]{1,0:T(8,128)}, f32[520,256]{1,0:T(8,128)S(1)}, u32[]{:S(2)}) copy-start(f32[520,256]{1,0:T(8,128)S(1)} %collective-permute-done.10.refs_2_) | copy-start | bytes 1597444
  (2 other events, 15.1 us)
